TPU v7x, 32 devices: a whole 2x2x4 slice. The times are simulated.
32 devices in a mesh: groups: 2 (over x), tensor: 16 (over z, y, core).
Axes of the slice: x: 2, y: 2, z: 4, core: 2. Of those that a mesh axis runs over, the one named last changes fastest.
Arguments:
- tokens: bfloat16 [256, 8192], P(('groups', 'tensor')), parts along dimension 0, may hold values from -6 to 6
- gate_weight: bfloat16 [8192, 28672], P(None, 'tensor'), may hold values from -0.0625 to 0.0625
- up_weight: bfloat16 [8192, 28672], P(None, 'tensor'), may hold values from -0.0625 to 0.0625
- adapter_down_weight: bfloat16 [16, 8192, 64], P('tensor'), may hold values from -0.0625 to 0.0625
- adapter_up_weight: bfloat16 [16, 64, 28672], P(None, None, 'tensor'), may hold values from -0.75 to 0.75
- token_adapter_index: int32 [256, 1], P(('groups', 'tensor')), parts along dimension 0, may hold values from 0 to 15; in each aligned block of 128 rows (0 to 127, 128 to 255, ...) at most 16 rows name the same one
- adapter_slot_index: int32 [16], replicated, may hold values from 0 to 15, each once
Outputs:
- hidden: bfloat16 [256, 28672], P('groups', 'tensor'), parts along dimension 0
There are 2 independent parts, one for each index of `groups`. A program takes and returns all parts, laid end to end along the dimension named above; an argument that names none is the same for every part. Nothing has to cross between parts.
Inputs may be any that keep to these rules, and one draw needn't show every extreme that they name: `token_adapter_index`: in every draw at most 16 of all 128 tokens use one adapter, and some adapter is used by exactly 16 tokens; every adapter is used by some token. `adapter_slot_index`: A permutation; slot s is stored on the device of index s along tensor.
All inputs are finite; a program needn't handle non-finite values.
Results may differ from a plain program's by a relative error of at most 0.0039.
Values may be sent and summed in bfloat16 or wider, within the bound.
No kernel may reach another device: no remote copies, remote signals or barrier semaphores. Data moves between devices by JAX's collectives and lax.ppermute only.
A program may use at most 192 MiB of HBM per device.

v0:
```python
import math
import jax
import jax.numpy as jnp
from jax import lax
from jax.sharding import PartitionSpec as P


def body(
    tokens,
    gate_weight,
    up_weight,
    adapter_down_weight,
    adapter_up_weight,
    token_adapter_index,
    adapter_slot_index,
):
    me = lax.axis_index("tensor")
    hidden_per_device = gate_weight.shape[1]
    all_ids = lax.all_gather(token_adapter_index, "tensor", axis=0, tiled=True)[:, 0]
    total = all_ids.shape[0]
    resident_weight = adapter_slot_index.shape[0]
    table_hits = all_ids[:, None] == jnp.arange(resident_weight, dtype=jnp.int32)[None, :]
    slot_of = jnp.sum(jnp.where(table_hits, adapter_slot_index[None, :], 0), axis=1)
    local_portion = lax.all_gather(tokens, "tensor", axis=0, tiled=True)
    mine = slot_of == me
    reduced_input = jnp.dot(
        local_portion, adapter_down_weight[0], preferred_element_type=jnp.float32
    )
    reduced_input = jnp.where(mine[:, None], reduced_input, 0.0)
    products = jnp.concatenate(
        [
            jnp.dot(local_portion, gate_weight, preferred_element_type=jnp.float32),
            jnp.dot(local_portion, up_weight, preferred_element_type=jnp.float32),
            reduced_input,
        ],
        axis=1,
    )
    gate = products[:, :hidden_per_device]
    up = products[:, hidden_per_device : 2 * hidden_per_device]
    low_part = products[:, 2 * hidden_per_device :]
    adapter_delta = lax.psum(low_part, "tensor").astype(jnp.bfloat16)
    device_position = adapter_delta.shape[1]
    up_weight_slice = adapter_up_weight.reshape(
        resident_weight * device_position, hidden_per_device
    )
    block = math.gcd(total, 256)
    low_blocks = adapter_delta.reshape(total // block, block, device_position)
    slot_blocks = slot_of.reshape(total // block, block)
    slot_range = jnp.arange(resident_weight, dtype=jnp.int32)

    def lift(args):
        reduced_input, selected_slot = args
        hits = selected_slot[:, None, None] == slot_range[None, :, None]
        spread = jnp.where(hits, reduced_input[:, None, :], jnp.zeros((), jnp.bfloat16)).reshape(
            reduced_input.shape[0], resident_weight * device_position
        )
        return jnp.dot(spread, up_weight_slice, preferred_element_type=jnp.float32)

    delta = lax.map(lift, (low_blocks, slot_blocks)).reshape(total, hidden_per_device)
    return (jax.nn.silu(gate) * (up + delta)).astype(jnp.bfloat16)


def solution(mesh):
    in_specs = (
        P(("groups", "tensor"), None),
        P(None, "tensor"),
        P(None, "tensor"),
        P("tensor", None, None),
        P(None, None, "tensor"),
        P(("groups", "tensor"), None),
        P(),
    )
    out_specs = P("groups", "tensor")
    return jax.shard_map(body, mesh=mesh, in_specs=in_specs, out_specs=out_specs, check_vma=False)
```

profile of v0, /device:TPU:0, one launch (start us, length us, event | category | flops | bytes accessed | tf_op | source)
XLA Modules:
  0.0 151.4 jit_solution(16022517166369663602)
XLA Ops:
  6.5 0.0 copy-start
  6.5 0.0 all-gather.2.cloned.1.call-start
  6.5 0.7 all-gather.2.cloned.1.call-update
  7.3 1.2 dynamic-slice.2
  9.2 0.8 bitcast_dynamic-update-slice_fusion
  9.9 13.8 %all-reduce = s32[128]{0:T(128)S(1)} all-reduce(s32[128]{0:T(128)S(1)} %bitcast_dynamic-update-slice_fusion), channel_id=1, replica_groups=mesh['groups'=2,'tensor'=16] {'tensor'}, use_global_device_ids=true, to_apply=%add | all-reduce | flops 128 | bytes 1024
  23.7 0.7 select_reduce_fusion
  24.5 29.1 %all-gather.2.cloned.1.call-done = bf16[128,8192]{1,0:T(8,128)(2,1)} async-done(((bf16[8,8192]{1,0:T(8,128)(2,1)}), bf16[128,8192]{1,0:T(8,128)(2,1)}) %all-gather.2.cloned.1.call-update) | async-done | bytes 2097168 | tf_op jit(solution)/shard_map/all_gather | solution.py:24
  53.7 0.0 copy-done
  53.7 0.0 copy-start.2
  53.7 2.6 %convolution_select_fusion = f32[128,64]{0,1:T(8,128)S(1)} fusion(bf16[128,8192]{1,0:T(8,128)(2,1)} %all-gather.2.cloned.1.call-done, bf16[1,8192,64]{1,2,0:T(8,128)(2,1)S(1)} %copy-done, pred[128]{0:T(512)(128)(4,1)S(1)} %broadcast_compare_fusion), kind=kOutput, calls=%fused_computation.4 | convolution fusion | flops 134225920 | bytes 3178624 | tf_op jit(solution)/shard_map/dot_general | solution.py:26
  56.2 59.5 %psum.7 = bf16[128,64]{0,1:T(8,128)(2,1)S(1)} all-reduce(f32[128,64]{0,1:T(8,128)S(1)} %convolution_select_fusion), channel_id=1, replica_groups=mesh['groups'=2,'tensor'=16] {'tensor'}, use_global_device_ids=true, to_apply=%region_1.2 | all-reduce | flops 8192 | bytes 49152 | tf_op jit(solution)/shard_map/psum | solution.py:41
  115.7 2.7 %convolution_bitcast_fusion = f32[128,1792]{1,0:T(8,128)S(1)} fusion(bf16[16,64,1792]{2,1,0:T(8,128)(2,1)} %param.11, pred[128,16]{0,1:T(8,128)(4,1)S(1)} %iota_compare_fusion, bf16[128,64]{0,1:T(8,128)(2,1)S(1)} %psum.7), kind=kOutput, calls=%fused_computation | convolution fusion | flops 469893120 | bytes 4605952 | tf_op jit(solution)/shard_map/while/body/eval_jaxpr/dot_general | solution.py:57
  118.4 0.0 copy-done.2
  118.4 11.7 %fusion.8 = f32[128,1792]{1,0:T(8,128)S(1)} fusion(bf16[128,8192]{1,0:T(8,128)(2,1)S(1)} %copy-done.2, bf16[8192,1792]{1,0:T(8,128)(2,1)} %param.8), kind=kOutput, calls=%fused_computation.16 | convolution fusion | flops 3758096384 | bytes 32374784 | tf_op jit(solution)/shard_map/dot_general | solution.py:32
  130.2 0.0 copy-start.1
  130.2 14.4 %fusion.1 = bf16[128,1792]{1,0:T(8,128)(2,1)} fusion(f32[128,1792]{1,0:T(8,128)S(1)} %convolution_bitcast_fusion, bf16[128,8192]{1,0:T(8,128)(2,1)S(1)} %copy-done.2, bf16[8192,1792]{1,0:T(8,128)(2,1)} %param.9, f32[128,1792]{1,0:T(8,128)S(1)} %fusion.8), kind=kOutput, calls=%fused_computation.3 | convolution fusion | flops 3759702016 | bytes 33751040 | tf_op jit(solution)/shard_map/dot_general | solution.py:33
  144.5 0.0 copy-done.1
  (3 shorter events, 0.0 us)
Async XLA Ops:
  6.5 47.1 %copy-start = (bf16[1,8192,64]{1,2,0:T(8,128)(2,1)S(1)}, bf16[1,8192,64]{1,2,0:T(8,128)(2,1)}, u32[]{:S(2)}) copy-start(bf16[1,8192,64]{1,2,0:T(8,128)(2,1)} %param.10) | copy-start | bytes 3145732
  6.5 47.1 %all-gather.2.cloned.1.call-start = ((), (), s32[]{:S(2)}) async-start(), calls=%async_computation | async-start | bytes 2228224 | tf_op jit(solution)/shard_map/all_gather | solution.py:24
  53.7 64.8 %copy-start.2 = (bf16[128,8192]{1,0:T(8,128)(2,1)S(1)}, bf16[128,8192]{1,0:T(8,128)(2,1)}, u32[]{:S(2)}) copy-start(bf16[128,8192]{1,0:T(8,128)(2,1)} %all-gather.2.cloned.1.call-done) | copy-start | bytes 6291460
  130.2 14.4 %copy-start.1 = (bf16[1,8192,64]{1,2,0:T(8,128)(2,1)S(1)}, bf16[1,8192,64]{1,2,0:T(8,128)(2,1)}, u32[]{:S(2)}) copy-start(bf16[1,8192,64]{1,2,0:T(8,128)(2,1)} %param.10) | copy-start | bytes 3145732
Sparse Core Ops, SparseCore 0:
  9.5 44.0 all-gather.1
where the time goes:
time: 152 us; the launch traced here: 151 us
  blocking collectives  73.3 us (48%)
  matrix products  31.4 us (21%)
  waiting for transfers between devices  29.9 us (20%)
  between operations  14.1 us (9%)
  local copies, waits for them, and re-layouts  2.01 us (1%)
    psum x1, blocking collectives, body(): adapter_delta = lax.psum(low_part, 'tensor').astype(jnp.bfloat16)  59.5 us
    all_gather x1, waiting for transfers between devices, body(): local_portion = lax.all_gather(tokens, 'tensor', axis=0, tiled=True)  29.1 us
    dot_general x1, matrix products, body(): jnp.dot(local_portion, up_weight, preferred_element_type=jnp.float32)  14.4 us
    unnamed x1, blocking collectives  13.8 us
    dot_general x1, matrix products, body(): jnp.dot(local_portion, gate_weight, preferred_element_type=jnp.float32)  11.7 us
  transfers between devices with their start and end apart: 1, of which 1 were waited for; matrix products, arithmetic and copies ran while one was open for 2% of the time, Pallas kernels for 0%

commit v1 on v0

--- a/solution.py
+++ b/solution.py
@@ -38,7 +38,7 @@
     gate = products[:, :hidden_per_device]
     up = products[:, hidden_per_device : 2 * hidden_per_device]
     low_part = products[:, 2 * hidden_per_device :]
-    adapter_delta = lax.psum(low_part, "tensor").astype(jnp.bfloat16)
+    adapter_delta = jnp.sum(lax.all_gather(low_part, "tensor"), axis=0).astype(jnp.bfloat16)
     device_position = adapter_delta.shape[1]
     up_weight_slice = adapter_up_weight.reshape(
         resident_weight * device_position, hidden_per_device

time: 152 us -> 111 us (0.73)
  blocking collectives: 73.3 us -> 34.6 us
  matrix products: 31.4 us -> 29.3 us
    psum x1 -> x0, blocking collectives: 59.5 us -> none  [body(): adapter_delta = lax.psum(low_part, 'tensor').astype(jnp.bfloat16)]
    all_gather x0 -> x1, blocking collectives: none -> 20.7 us  [body(): lax.all_gather(low_part, 'tensor')]
    dot_general x1, matrix products: 2.71 us -> 0.67 us  [lift(): return jnp.dot(spread, up_weight_slice, preferred_element_type=jnp.float32)]
where the time goes in v1:
time: 111 us
  blocking collectives  34.6 us (31%)
  waiting for transfers between devices  29.9 us (27%)
  matrix products  29.3 us (26%)
  between operations  14.1 us (13%)
  local copies, waits for them, and re-layouts  2.11 us (2%)
    all_gather x1, waiting for transfers between devices, body(): local_portion = lax.all_gather(tokens, 'tensor', axis=0, tiled=True)  29.1 us
    all_gather x1, blocking collectives, body(): lax.all_gather(low_part, 'tensor')  20.7 us
    dot_general x1, matrix products, body(): jnp.dot(local_portion, up_weight, preferred_element_type=jnp.float32)  14.4 us
    unnamed x1, blocking collectives  13.8 us
    dot_general x1, matrix products, body(): jnp.dot(local_portion, gate_weight, preferred_element_type=jnp.float32)  11.7 us
    dot_general x1, matrix products, body(): jnp.dot(local_portion, adapter_down_weight[0], preferred_element_type=jnp...  2.58 us
  transfers between devices with their start and end apart: 1, of which 1 were waited for; matrix products, arithmetic and copies ran while one was open for 2% of the time, Pallas kernels for 0%

profile of v1, /device:TPU:0, one launch (start us, length us, event | category | flops | bytes accessed | tf_op | source)
XLA Modules:
  0.0 110.9 jit_solution(9689183251922081512)
XLA Ops:
  6.5 0.0 copy-start
  6.5 0.0 all-gather.3.cloned.1.call-start
  6.5 0.7 all-gather.3.cloned.1.call-update
  7.3 1.2 %dynamic-slice.2 = u32[1]{0:T(128)} dynamic-slice(u32[32]{0:T(128)} %constant.30, u32[]{:T(128)S(6)} %add.11), dynamic_slice_sizes={1} | dynamic-slice | bytes 12
  9.2 0.8 bitcast_dynamic-update-slice_fusion
  9.9 13.8 %all-reduce = s32[128]{0:T(128)S(1)} all-reduce(s32[128]{0:T(128)S(1)} %bitcast_dynamic-update-slice_fusion), channel_id=1, replica_groups=mesh['groups'=2,'tensor'=16] {'tensor'}, use_global_device_ids=true, to_apply=%add | all-reduce | flops 128 | bytes 1024
  23.7 0.7 select_reduce_fusion
  24.5 29.1 %all-gather.3.cloned.1.call-done = bf16[128,8192]{1,0:T(8,128)(2,1)} async-done(((bf16[8,8192]{1,0:T(8,128)(2,1)}), bf16[128,8192]{1,0:T(8,128)(2,1)}) %all-gather.3.cloned.1.call-update) | async-done | bytes 2097168 | tf_op jit(solution)/shard_map/all_gather | solution.py:24
  53.7 0.0 copy-done
  53.7 0.0 copy-start.3
  53.7 2.6 %convolution_select_fusion = f32[128,64]{0,1:T(8,128)S(1)} fusion(bf16[128,8192]{1,0:T(8,128)(2,1)} %all-gather.3.cloned.1.call-done, bf16[1,8192,64]{1,2,0:T(8,128)(2,1)S(1)} %copy-done, pred[128]{0:T(512)(128)(4,1)S(1)} %broadcast_compare_fusion), kind=kOutput, calls=%fused_computation.4 | convolution fusion | flops 134225920 | bytes 3178624 | tf_op jit(solution)/shard_map/dot_general | solution.py:26
  56.2 0.0 copy-start.2
  56.3 20.7 %all-gather = f32[2048,64]{0,1:T(8,128)S(1)} all-gather(f32[128,64]{0,1:T(8,128)S(1)} %convolution_select_fusion), channel_id=2, replica_groups=mesh['groups'=2,'tensor'=16] {'tensor'}, dimensions={0}, use_global_device_ids=true | all-gather | bytes 557056 | tf_op jit(solution)/shard_map/all_gather | solution.py:41
  77.0 0.1 copy.8
  77.1 0.1 bitcast_reduce_fusion
  77.2 0.0 copy-done.3
  77.2 0.7 convolution_bitcast_fusion
  77.9 0.0 copy-done.2
  77.9 11.7 %fusion.8 = f32[128,1792]{1,0:T(8,128)S(1)} fusion(bf16[128,8192]{1,0:T(8,128)(2,1)S(1)} %copy-done.2, bf16[8192,1792]{1,0:T(8,128)(2,1)} %param.8), kind=kOutput, calls=%fused_computation.17 | convolution fusion | flops 3758096384 | bytes 32374784 | tf_op jit(solution)/shard_map/dot_general | solution.py:32
  89.6 0.0 copy-start.1
  89.6 14.4 %fusion.1 = bf16[128,1792]{1,0:T(8,128)(2,1)} fusion(f32[128,1792]{1,0:T(8,128)S(1)} %convolution_bitcast_fusion, bf16[128,8192]{1,0:T(8,128)(2,1)S(1)} %copy-done.2, bf16[8192,1792]{1,0:T(8,128)(2,1)} %param.9, f32[128,1792]{1,0:T(8,128)S(1)} %fusion.8), kind=kOutput, calls=%fused_computation.3 | convolution fusion | flops 3759702016 | bytes 33751040 | tf_op jit(solution)/shard_map/dot_general | solution.py:33
  104.0 0.0 copy-done.1
  (3 shorter events, 0.0 us)
Async XLA Ops:
  6.5 47.1 %copy-start = (bf16[1,8192,64]{1,2,0:T(8,128)(2,1)S(1)}, bf16[1,8192,64]{1,2,0:T(8,128)(2,1)}, u32[]{:S(2)}) copy-start(bf16[1,8192,64]{1,2,0:T(8,128)(2,1)} %param.10) | copy-start | bytes 3145732
  6.5 47.1 %all-gather.3.cloned.1.call-start = ((), (), s32[]{:S(2)}) async-start(), calls=%async_computation | async-start | bytes 2228224 | tf_op jit(solution)/shard_map/all_gather | solution.py:24
  53.7 23.5 %copy-start.3 = (bf16[16,64,1792]{2,1,0:T(8,128)(2,1)S(1)}, bf16[16,64,1792]{2,1,0:T(8,128)(2,1)}, u32[]{:S(2)}) copy-start(bf16[16,64,1792]{2,1,0:T(8,128)(2,1)} %param.11) | copy-start | bytes 11010052
  56.2 21.6 %copy-start.2 = (bf16[128,8192]{1,0:T(8,128)(2,1)S(1)}, bf16[128,8192]{1,0:T(8,128)(2,1)}, u32[]{:S(2)}) copy-start(bf16[128,8192]{1,0:T(8,128)(2,1)} %all-gather.3.cloned.1.call-done) | copy-start | bytes 6291460
  89.6 14.4 %copy-start.1 = (bf16[1,8192,64]{1,2,0:T(8,128)(2,1)S(1)}, bf16[1,8192,64]{1,2,0:T(8,128)(2,1)}, u32[]{:S(2)}) copy-start(bf16[1,8192,64]{1,2,0:T(8,128)(2,1)} %param.10) | copy-start | bytes 3145732
Sparse Core Ops, SparseCore 0:
  9.5 44.0 all-gather.2
